TPU v7x, 32 devices: a whole 2x2x4 slice. The times are simulated.
32 devices in a mesh: groups: 2 (over y), leaf: 4 (over z), state: 2 (over x), sub: 2 (over core).
Axes of the slice: x: 2, y: 2, z: 4, core: 2. Of those that a mesh axis runs over, the one named last changes fastest.
Arguments:
- sphere_coef: bfloat16 [12, 25, 2, 2, 4, 2048], P(None, None, None, None, None, ('groups', 'leaf', 'state', 'sub')), parts along dimension 5, may hold values from -6 to 6
- live_blocks: int32 [32], P(('groups', 'leaf', 'state', 'sub')), parts along dimension 0, may hold values from 1 to 4, as said below
- cluster: int32 [2048], P(('groups', 'leaf', 'state', 'sub')), parts along dimension 0, may hold values from 0 to 15
- leaf_parent: int32 [512], P(('groups', 'leaf', 'state', 'sub')), parts along dimension 0, may hold values from 0 to 1
- leaf_octant: int32 [512], P(('groups', 'leaf', 'state', 'sub')), parts along dimension 0, may hold values from 0 to 7
- box_octant: int32 [64], P(('groups', 'leaf', 'state', 'sub')), parts along dimension 0, may hold values from 0 to 7
- rotation: float32 [8, 2, 12, 25, 25], replicated, may hold values from -0.875 to 0.875
- axial_one: float32 [2, 25, 2, 12, 2, 12], replicated, may hold values from -0.3125 to 0.3125
- axial_two: float32 [2, 25, 2, 12, 2, 12], replicated, may hold values from -0.3125 to 0.3125
- owner_rotation: float32 [8, 2, 12, 25, 25], P(('groups', 'leaf')), parts along dimension 0, may hold values from -0.875 to 0.875
- owner_axial: float32 [8, 2, 25, 2, 128, 2, 12], P(('groups', 'leaf'), None, None, None, ('state', 'sub')), parts along dimension 0, may hold values from -0.875 to 0.875
- owner_angle: float32 [8], P('groups'), parts along dimension 0, may hold values from -3.140625 to 3.140625
- turn_table: bfloat16 [8, 128, 25, 256], P(('groups', 'leaf'), ('state', 'sub')), parts along dimension 0, may hold values from -0.625 to 0.625
- angular_table: bfloat16 [256, 128, 32], P('leaf', ('state', 'sub')), may hold values from -0.375 to 0.375
Outputs:
- far_field: float32 [32, 4, 2, 2, 2048], P(('groups', 'leaf', 'state', 'sub')), parts along dimension 0
There are 2 independent parts, one for each index of `groups`. A program takes and returns all parts, laid end to end along the dimension named above; an argument that names none is the same for every part. Nothing has to cross between parts.
Inputs may be any that keep to these rules, and one draw needn't show every extreme that they name: `live_blocks`: live blocks of 16 sphere slots on each device; some device has all 4 live in every draw.
All inputs are finite; a program needn't handle non-finite values.
Results may differ from a plain program's by a relative error of at most 0.018.
Values may be sent and summed in bfloat16 or wider, within the bound.
No kernel may reach another device: no remote copies, remote signals or barrier semaphores. Data moves between devices by JAX's collectives and lax.ppermute only.
A program may use at most 64 MiB of HBM per device.

v0:
```python
import math
import jax
import jax.numpy as jnp
from jax import lax
from jax.sharding import PartitionSpec as P

STATES = 4
SBLK = 4
PHI = 2048


def complex_join(first, second, half):
    real = first[..., :half] - second[..., half:]
    imag = first[..., half:] + second[..., :half]
    return jnp.concatenate([real, imag], axis=-1)


def turn_select(vectors, rotation, octants, backward):
    degrees, orders, width = vectors.shape
    if backward:
        mats = jnp.transpose(rotation, (1, 2, 0, 4, 3))
        sign = -1.0
    else:
        mats = jnp.transpose(rotation, (1, 2, 0, 3, 4))
        sign = 1.0
    mats = mats.reshape(2, degrees, 8 * orders, orders)
    first = jnp.einsum("lQp,lpC->lQC", mats[0], vectors, precision=lax.Precision.HIGHEST)
    second = sign * jnp.einsum("lQp,lpC->lQC", mats[1], vectors, precision=lax.Precision.HIGHEST)
    joined = complex_join(first, second, width // 2).reshape(degrees, 8, orders, width)
    count = octants.shape[0]
    chosen = (octants[None, :] == jnp.arange(8, dtype=jnp.int32)[:, None]).astype(jnp.float32)
    column_mask = jnp.tile(chosen, (1, width // count))
    return jnp.sum(joined * column_mask[None, :, None, :], axis=1)


def axial_apply(vectors, axial):
    degrees, orders, width = vectors.shape
    rest = width // 4
    moved = vectors.reshape(degrees, orders, 2, 2, rest)
    moved = jnp.transpose(moved, (1, 3, 0, 2, 4)).reshape(orders, 2 * degrees, 2 * rest)
    mats = axial.reshape(2, orders, 2 * degrees, 2 * degrees)
    first = jnp.einsum("qab,qbC->qaC", mats[0], moved, precision=lax.Precision.HIGHEST)
    second = jnp.einsum("qab,qbC->qaC", mats[1], moved, precision=lax.Precision.HIGHEST)
    joined = complex_join(first, second, rest).reshape(orders, 2, degrees, 2, rest)
    return jnp.transpose(joined, (2, 0, 3, 1, 4)).reshape(degrees, orders, width)


def move_expansion(vectors, octants, rotation, axial):
    turned = turn_select(vectors, rotation, octants, False)
    return turn_select(axial_apply(turned, axial), rotation, octants, True)


def local_boxes(
    sphere_block,
    live_count,
    cluster,
    leaf_parent,
    leaf_octant,
    box_octant,
    rotation,
    axial_one,
    axial_two,
):
    degrees, orders = (sphere_block.shape[0], sphere_block.shape[1])
    channel = sphere_block.shape[2] * sphere_block.shape[3] * sphere_block.shape[4]
    slots = sphere_block.shape[-1]
    per_block = slots // SBLK
    alive = jnp.arange(slots, dtype=jnp.int32) // per_block < live_count
    leaf_total = leaf_parent.shape[0]
    member = (
        (cluster[:, None] == jnp.arange(leaf_total, dtype=jnp.int32)[None, :]) & alive[:, None]
    ).astype(jnp.bfloat16)
    ident = jnp.eye(channel, dtype=jnp.bfloat16)
    spread = (ident[:, None, :, None] * member[None, :, None, :]).reshape(
        channel * slots, channel * leaf_total
    )
    leaves = jnp.dot(
        sphere_block.reshape(degrees * orders, channel * slots),
        spread,
        preferred_element_type=jnp.float32,
    ).reshape(degrees, orders, channel * leaf_total)
    moved = move_expansion(leaves, leaf_octant, rotation, axial_one)
    box_total = box_octant.shape[0]
    parents = (leaf_parent[:, None] == jnp.arange(box_total, dtype=jnp.int32)[None, :]).astype(
        jnp.float32
    )
    wide_ident = jnp.eye(channel, dtype=jnp.float32)
    wide_parents = (wide_ident[:, None, :, None] * parents[None, :, None, :]).reshape(
        channel * leaf_total, channel * box_total
    )
    boxes = jnp.einsum("lpC,CD->lpD", moved, wide_parents, precision=lax.Precision.HIGHEST)
    outer = move_expansion(boxes, box_octant, rotation, axial_two)
    return outer.reshape(degrees, orders, channel, box_total).sum(-1)


def owner_frame(owner_sum, owner_turn, owner_shift):
    degrees, orders, width = owner_sum.shape
    states = width // 4
    first = jnp.einsum("lqp,lpC->lqC", owner_turn[0], owner_sum, precision=lax.Precision.HIGHEST)
    second = jnp.einsum("lqp,lpC->lqC", owner_turn[1], owner_sum, precision=lax.Precision.HIGHEST)
    turned = complex_join(first, second, width // 2)
    moved = turned.reshape(degrees, orders, 2, 2, states)
    moved = jnp.transpose(moved, (1, 3, 0, 2, 4)).reshape(orders, 2 * degrees, 2 * states)
    root_degrees = owner_shift.shape[3]
    mats = owner_shift.reshape(2, orders, 2 * root_degrees, 2 * degrees)
    first = jnp.einsum("qab,qbC->qaC", mats[0], moved, precision=lax.Precision.HIGHEST)
    second = jnp.einsum("qab,qbC->qaC", mats[1], moved, precision=lax.Precision.HIGHEST)
    joined = complex_join(first, second, states).reshape(orders, 2, root_degrees, 2, states)
    framed = jnp.transpose(joined, (2, 1, 3, 4, 0)).reshape(root_degrees, 4 * states, orders)
    return framed.astype(jnp.bfloat16)


def rotate_back(framed, functions, azimuth, half_orders):
    root_degrees, width = (framed.shape[0], framed.shape[1])
    states = width // 4
    orders_here = functions.shape[2]
    values = jnp.einsum("nCm,nmj->nCj", framed, functions, preferred_element_type=jnp.float32)
    values = values.reshape(root_degrees, 2, 2, states, orders_here)
    order_values = (jnp.arange(orders_here, dtype=jnp.int32) - half_orders).astype(jnp.float32)
    cosine = jnp.cos(order_values * azimuth)
    sine = jnp.sin(order_values * azimuth)
    real_part = cosine * values[:, :, 0] + sine * values[:, :, 1]
    imag_part = cosine * values[:, :, 1] - sine * values[:, :, 0]
    joined = jnp.stack([real_part, imag_part], axis=2)
    return jnp.transpose(joined, (4, 1, 2, 3, 0)).reshape(orders_here, 4 * states * root_degrees)


def legendre_field(root_coef, table):
    orders_here, root_degrees = (table.shape[0], table.shape[1])
    lat_total = table.shape[2] // 2
    rows = root_coef.shape[1] // root_degrees
    states = rows // 4
    half = rows // 2
    blocks = jnp.einsum(
        "jrn,jnK->jrK",
        root_coef.reshape(orders_here, rows, root_degrees),
        table,
        preferred_element_type=jnp.float32,
    )
    theta_part = blocks[:, :half, :lat_total] + blocks[:, half:, lat_total:]
    cross = blocks[:, :half, lat_total:] + blocks[:, half:, :lat_total]
    phi_part = jnp.concatenate([-cross[:, states:], cross[:, :states]], axis=1)
    return jnp.concatenate([theta_part, phi_part], axis=1)


def phase_table(orders, longitudes):
    order_ids = jnp.arange(orders, dtype=jnp.int32) - orders // 2
    column = jnp.arange(2 * longitudes, dtype=jnp.int32)
    along = column % longitudes
    quarter = (column // longitudes).astype(jnp.float32)
    remainder = jnp.mod(order_ids[:, None] * along[None, :], longitudes)
    phase = remainder.astype(jnp.float32) * (2.0 * math.pi / longitudes) - quarter[None, :] * (
        0.5 * math.pi
    )
    return jnp.cos(phase).astype(jnp.bfloat16)


def synthesize(spectrum, longitudes, states):
    orders = spectrum.shape[1]
    table = phase_table(orders, longitudes)
    product = jnp.dot(spectrum, table, preferred_element_type=jnp.float32)
    product = product.reshape(2, 2, states, -1, 2 * longitudes)
    real_part = product[:, 0, :, :, :longitudes] - product[:, 1, :, :, longitudes:]
    imag_part = product[:, 0, :, :, longitudes:] + product[:, 1, :, :, :longitudes]
    joined = jnp.stack([real_part, imag_part], axis=3)
    return jnp.transpose(joined, (2, 1, 0, 3, 4)) * (1.0 / math.sqrt(orders))


def on_device(
    sphere_coef,
    live_blocks,
    cluster,
    leaf_parent,
    leaf_octant,
    box_octant,
    rotation,
    axial_one,
    axial_two,
    owner_rotation,
    owner_axial,
    owner_angle,
    turn_table,
    angular_table,
):
    partial_owner = local_boxes(
        sphere_coef,
        live_blocks[0],
        cluster,
        leaf_parent,
        leaf_octant,
        box_octant,
        rotation,
        axial_one,
        axial_two,
    )
    owner_sum = lax.psum(partial_owner, ("state", "sub"))
    framed = owner_frame(owner_sum, owner_rotation[0], owner_axial[0])
    leaf_size = lax.axis_size("leaf")
    orders = turn_table.shape[3]
    half_orders = orders // 2
    own_orders = orders // leaf_size
    own_azimuth = owner_angle[lax.axis_index("leaf")]
    piece = turn_table[0]
    root = lax.psum_scatter(
        rotate_back(framed, piece, own_azimuth, half_orders),
        "leaf",
        scatter_dimension=0,
        tiled=True,
    )
    root_coef = root.astype(jnp.bfloat16)
    field = legendre_field(root_coef, angular_table)
    channel = field.shape[1]
    group_size = lax.axis_size("state") * lax.axis_size("sub")
    lat_rows = field.shape[2] // (leaf_size * group_size)
    shaped = field.reshape(own_orders, channel, leaf_size, group_size, lat_rows)
    shaped = jnp.transpose(shaped, (3, 2, 1, 4, 0)).reshape(
        group_size, leaf_size, channel * lat_rows * own_orders
    )
    summed = lax.psum_scatter(
        shaped.astype(jnp.bfloat16), ("state", "sub"), scatter_dimension=0, tiled=True
    )
    moved = lax.all_to_all(summed, "leaf", split_axis=1, concat_axis=2, tiled=True)
    spectrum = moved.reshape(leaf_size, channel, lat_rows, own_orders)
    spectrum = jnp.transpose(spectrum, (1, 2, 0, 3)).reshape(channel * lat_rows, orders)
    return synthesize(spectrum, PHI, STATES)


def solution(mesh):
    return jax.shard_map(
        on_device,
        mesh=mesh,
        in_specs=(
            P(None, None, None, None, None, ("groups", "leaf", "state", "sub")),
            P(("groups", "leaf", "state", "sub")),
            P(("groups", "leaf", "state", "sub")),
            P(("groups", "leaf", "state", "sub")),
            P(("groups", "leaf", "state", "sub")),
            P(("groups", "leaf", "state", "sub")),
            P(),
            P(),
            P(),
            P(("groups", "leaf"), None, None, None, None),
            P(("groups", "leaf"), None, None, None, ("state", "sub"), None, None),
            P("groups"),
            P(("groups", "leaf"), ("state", "sub"), None, None),
            P("leaf", ("state", "sub"), None),
        ),
        out_specs=P(("groups", "leaf", "state", "sub"), None, None, None, None),
        check_vma=False,
    )
```

profile of v0, /device:TPU:0, one launch (start us, length us, event | category | flops | bytes accessed | tf_op | source)
XLA Modules:
  0.0 170.0 jit_solution(8647744957523525391)
XLA Ops:
  6.5 0.6 fusion.33
  7.1 4.5 %fusion.46 = (f32[1,12,8,25,25]{4,0,3,1,2:T(1,128)S(1)}, f32[1,12,8,25,25]{4,0,3,1,2:T(1,128)S(1)}) fusion(f32[2,12,8,25,25]{4,0,3,1,2:T(2,128)} %bitcast.182), kind=kLoop, calls=%fused_computation.129 | loop fusion | bytes 960000 | tf_op jit(solution)/shard_map/slice | solution.py:27
  11.7 2.4 %copy.163 = f32[1,12,8,25,25]{3,2,4,1,0:T(8,128)} copy(f32[1,12,8,25,25]{4,0,3,1,2:T(1,128)S(1)} %get-tuple-element.12) | data formatting | bytes 480000 | tf_op jit(solution)/shard_map/slice | solution.py:28
  14.1 2.4 %squeeze.61 = f32[12,200,25]{1,2,0:T(8,128)} reshape(f32[1,12,8,25,25]{3,2,4,1,0:T(8,128)} %copy.163) | data formatting | bytes 480000 | tf_op jit(solution)/shard_map/squeeze | solution.py:28
  17.4 0.7 mul.178
  18.1 2.6 %reshape.344 = bf16[300,1024]{1,0:T(8,128)(2,1)S(1)} reshape(bf16[12,25,2,2,4,64]{5,4,3,2,1,0:T(4,128)(2,1)} %param.14) | data formatting | bytes 1228800 | tf_op jit(solution)/shard_map/reshape | solution.py:78
  21.2 1.1 copy.162
  22.7 3.3 %convolution_bitcast_fusion.2 = f32[12,200,256]{2,1,0:T(8,128)S(1)} fusion(f32[12,25,256]{2,1,0:T(8,128)S(1)} %reshape.345, f32[12,200,25]{1,2,0:T(8,128)} %squeeze.61), kind=kOutput, calls=%fused_computation.26 | convolution fusion | flops 184320000 | bytes 3004800 | tf_op jit(solution)/shard_map/lQp,lpC->lQC/dot_general | solution.py:28
  26.0 2.2 %convolution_bitcast_fusion.3 = f32[12,200,256]{2,1,0:T(8,128)S(1)} fusion(f32[12,25,256]{2,1,0:T(8,128)S(1)} %reshape.345, f32[12,200,25]{1,2,0:T(8,128)S(1)} %squeeze.60), kind=kOutput, calls=%fused_computation.27 | convolution fusion | flops 184320000 | bytes 3004800 | tf_op jit(solution)/shard_map/lQp,lpC->lQC/dot_general | solution.py:27
  28.4 1.6 pad_maximum_fusion
  30.1 2.5 %reshape.346 = f32[12,8,25,256]{3,2,1,0:T(8,128)S(1)} reshape(f32[12,200,256]{2,1,0:T(8,128)} %pad_maximum_fusion) | data formatting | bytes 4915200 | tf_op jit(solution)/shard_map/reshape | solution.py:29
  32.5 0.7 fusion.37
  33.2 0.6 tile.8
  33.8 1.5 tile.9
  35.4 1.9 %multiply_reduce_fusion.1 = f32[12,25,256]{2,1,0:T(8,128)} fusion(f32[12,8,25,256]{3,2,1,0:T(8,128)S(1)} %reshape.346, f32[8,256]{1,0:T(8,128)} %tile.9), kind=kLoop, calls=%fused_computation.13 | loop fusion | flops 1152000 | bytes 2772992 | tf_op jit(solution)/shard_map/reduce_sum | solution.py:33
  37.2 1.4 reshape.347
  39.4 0.7 copy.206
  40.4 1.1 copy.205
  41.8 0.6 convolution_bitcast_fusion.8
  42.5 0.6 convolution_bitcast_fusion.9
  43.5 1.2 reshape.349
  44.7 2.2 %copy.169 = f32[12,25,2,2,64]{4,3,2,1,0:T(2,128)} copy(f32[12,25,2,2,64]{4,2,0,3,1:T(2,128)} %bitcast.184) | data formatting | bytes 614400 | tf_op jit(solution)/shard_map/transpose | solution.py:45
  46.9 1.5 reshape.350
  48.4 2.9 %fusion.45 = (f32[1,12,8,25,25]{3,0,4,1,2:T(1,128)S(1)}, f32[1,12,8,25,25]{3,0,4,1,2:T(1,128)}) fusion(f32[2,12,8,25,25]{3,0,4,1,2:T(2,128)S(1)} %bitcast.183), kind=kLoop, calls=%fused_computation.128 | loop fusion | bytes 960000 | tf_op jit(solution)/shard_map/slice | solution.py:27
  51.5 1.1 squeeze.64
  53.1 3.3 %convolution_bitcast_fusion.1 = f32[12,200,256]{2,1,0:T(8,128)S(1)} fusion(f32[12,25,256]{2,1,0:T(8,128)S(1)} %reshape.350, f32[12,200,25]{1,2,0:T(8,128)} %squeeze.64), kind=kOutput, calls=%fused_computation.25 | convolution fusion | flops 184320000 | bytes 3004800 | tf_op jit(solution)/shard_map/lQp,lpC->lQC/dot_general | solution.py:27
  56.5 2.2 %multiply_bitcast_fusion = f32[12,200,256]{2,1,0:T(8,128)S(1)} fusion(f32[12,25,256]{2,1,0:T(8,128)S(1)} %reshape.350, f32[12,200,25]{1,2,0:T(8,128)S(1)} %squeeze.65), kind=kOutput, calls=%fused_computation.16 | convolution fusion | flops 184934400 | bytes 3004800 | tf_op jit(solution)/shard_map/lQp,lpC->lQC/dot_general | solution.py:28
  58.9 1.6 pad_maximum_fusion.1
  60.5 2.6 %reshape.351 = f32[12,8,25,256]{3,2,1,0:T(8,128)S(1)} reshape(f32[12,200,256]{2,1,0:T(8,128)} %pad_maximum_fusion.1) | data formatting | bytes 4915200 | tf_op jit(solution)/shard_map/reshape | solution.py:29
  63.2 1.9 %multiply_reduce_fusion = f32[12,25,256]{2,1,0:T(8,128)} fusion(f32[12,8,25,256]{3,2,1,0:T(8,128)S(1)} %reshape.351, f32[8,256]{1,0:T(8,128)} %tile.9), kind=kLoop, calls=%fused_computation.12 | loop fusion | flops 1152000 | bytes 2772992 | tf_op jit(solution)/shard_map/reduce_sum | solution.py:33
  65.3 2.0 %fusion.51 = f32[12,25,32]{1,2,0:T(8,128)S(1)} fusion(f32[12,25,256]{2,1,0:T(8,128)} %multiply_reduce_fusion, f32[256,32,1]{0,1,2:T(8,128)S(1)} %reshape.365), kind=kOutput, calls=%fused_computation.136 | convolution fusion | flops 29491200 | bytes 378368 | tf_op jit(solution)/shard_map/lpC,CD->lpD/dot_general | solution.py:91
  67.3 1.5 convolution_bitcast_fusion.6
  68.8 1.5 convolution_bitcast_fusion.5
  70.4 0.5 reshape.352
  71.0 0.5 multiply_reduce_fusion.3
  71.8 0.7 copy.208
  72.8 0.7 copy.207
  73.8 0.6 convolution_bitcast_fusion.10
  74.4 0.6 convolution_bitcast_fusion.11
  75.3 0.5 convolution_bitcast_fusion.4
  75.8 0.5 fusion.15
  76.4 0.5 reshape.357
  76.9 0.5 multiply_reduce_fusion.2
  77.7 13.9 %psum.7 = f32[12,25,16]{1,2,0:T(8,128)S(1)} all-reduce(f32[12,25,16]{1,2,0:T(8,128)S(1)} %reduce_sum.49), channel_id=1, replica_groups=mesh['groups'=2,'leaf'=4,'state'=2,'sub'=2] {'state','sub'}, use_global_device_ids=true, to_apply=%region_5.6 | all-reduce | flops 4800 | bytes 38400 | tf_op jit(solution)/shard_map/psum | solution.py:196
  91.6 1.4 fusion.50
  93.0 0.4 convolution_bitcast_fusion.14
  93.4 0.4 convolution_bitcast_fusion.15
  95.9 0.4 convolution_bitcast_fusion.13
  97.5 0.6 dynamic_slice.3
  98.0 0.7 fusion.38
  98.9 1.0 copy.210
  99.9 0.8 copy.195
  100.7 0.6 dynamic-slice
  101.3 20.8 %reduce-scatter.4.cloned.1.call-done = f32[64,512]{1,0:T(8,128)} async-done(((f32[256,512]{1,0:T(8,128)}), f32[64,512]{1,0:T(8,128)}) %reduce-scatter.4.cloned.1.call-update) | async-done | bytes 131088
  122.0 1.0 copy.211
  124.5 10.3 %all-reduce = bf16[4,4,1024]{2,1,0:T(4,128)(2,1)S(1)} all-reduce(bf16[4,4,1024]{2,1,0:T(4,128)(2,1)S(1)} %copy.209), channel_id=3, replica_groups=mesh['groups'=2,'leaf'=4,'state'=2,'sub'=2] {'state','sub'}, use_global_device_ids=true, to_apply=%region_7.8.clone | all-reduce | flops 16384 | bytes 65536
  134.7 0.7 constant_dynamic-slice_fusion
  135.4 0.5 broadcast.208
  135.9 0.7 reduce.2
  136.6 0.6 reshape.377
  137.3 3.5 %all-to-all-start = ((bf16[4,2,512]{2,1,0:T(2,128)(2,1)}), bf16[4,2,512]{2,1,0:T(2,128)(2,1)S(1)}, u32[]{:S(2)}, u32[]{:S(2)}) async-start(bf16[4,2,512]{2,1,0:T(2,128)(2,1)} %reshape.377), calls=%async_computation | async-start | bytes 16384 | tf_op jit(solution)/shard_map/all_to_all | solution.py:222
  140.7 5.3 %all-to-all-done = bf16[4,2,512]{2,1,0:T(2,128)(2,1)S(1)} async-done(((bf16[4,2,512]{2,1,0:T(2,128)(2,1)}), bf16[4,2,512]{2,1,0:T(2,128)(2,1)S(1)}, u32[]{:S(2)}, u32[]{:S(2)}) %all-to-all-start) | async-done | bytes 8224 | tf_op jit(solution)/shard_map/all_to_all | solution.py:222
  146.3 15.7 %convolution_bitcast_fusion = f32[2,2,4,1,4096]{4,2,1,0,3:T(4,128)S(1)} fusion(bf16[2,2,4,256]{3,2,1,0:T(4,128)(2,1)S(1)} %dot_general.132, f32[4096]{0:T(1024)S(1)} %fusion.28, s32[4096]{0:T(1024)S(1)} %add_select_fusion.2, s32[256]{0:T(256)S(1)} %iota_add_fusion), kind=kOutput, calls=%fused_computation.5 | convolution fusion | flops 50331648 | bytes 304128 | tf_op jit(solution)/shard_map/dot_general | solution.py:161
  162.1 0.8 copy.202
  (113 shorter events, 10.7 us)
Async XLA Ops:
  6.5 90.2 %copy-start = (bf16[1,32,25,256]{3,1,2,0:T(8,128)(2,1)S(1)}, bf16[1,32,25,256]{3,1,2,0:T(8,128)(2,1)}, u32[]{:S(2)}) copy-start(bf16[1,32,25,256]{3,1,2,0:T(8,128)(2,1)} %param.26) | copy-start | bytes 1228804
  6.5 115.5 %reduce-scatter.4.cloned.1.call-start = ((), (), s32[]{:S(2)}) async-start(), calls=%async_computation.2 | async-start | bytes 655360
  11.7 5.5 %copy-start.12 = (s32[64]{0:T(128)S(1)}, s32[64]{0:T(128)}, u32[]{:S(2)}) copy-start(s32[64]{0:T(128)} %param.16) | copy-start | bytes 772
  22.7 5.5 %copy-start.3 = (f32[12,200,25]{1,2,0:T(8,128)}, f32[12,200,25]{1,2,0:T(8,128)S(1)}, u32[]{:S(2)}) copy-start(f32[12,200,25]{1,2,0:T(8,128)S(1)} %squeeze.60) | copy-start | bytes 720004
  37.2 2.1 %copy-start.8 = (f32[2,25,2,12,2,12]{1,4,5,3,2,0:T(2,128)S(1)}, f32[2,25,2,12,2,12]{1,4,5,3,2,0:T(2,128)}, u32[]{:S(2)}) copy-start(f32[2,25,2,12,2,12]{1,4,5,3,2,0:T(2,128)} %param.21) | copy-start | bytes 345604
  43.3 5.1 %copy-start.1 = (f32[8,2,12,25,25]{4,1,3,2,0:T(2,128)S(1)}, f32[8,2,12,25,25]{4,1,3,2,0:T(2,128)}, u32[]{:S(2)}) copy-start(f32[8,2,12,25,25]{4,1,3,2,0:T(2,128)} %param.20) | copy-start | bytes 1440004
  51.4 1.3 copy-start.2
  53.1 5.5 %copy-start.5 = (f32[12,200,25]{1,2,0:T(8,128)}, f32[12,200,25]{1,2,0:T(8,128)S(1)}, u32[]{:S(2)}) copy-start(f32[12,200,25]{1,2,0:T(8,128)S(1)} %squeeze.65) | copy-start | bytes 720004
  63.2 1.9 %copy-start.13 = (s32[16]{0:T(128)S(1)}, s32[16]{0:T(128)}, u32[]{:S(2)}) copy-start(s32[16]{0:T(128)} %param.17) | copy-start | bytes 196
  63.2 1.9 %copy-start.11 = (f32[16,16]{0,1:T(8,128)S(1)}, f32[16,16]{0,1:T(8,128)}, u32[]{:S(2)}) copy-start(f32[16,16]{0,1:T(8,128)} %fusion.33) | copy-start | bytes 3076
  68.8 2.1 %copy-start.14 = (s32[2]{0:T(128)S(1)}, s32[2]{0:T(128)}, u32[]{:S(2)}) copy-start(s32[2]{0:T(128)} %param.19) | copy-start | bytes 28
  70.4 1.4 copy-start.9
  72.8 2.5 %copy-start.4 = (f32[12,200,25]{1,2,0:T(8,128)S(1)}, f32[12,200,25]{1,2,0:T(8,128)}, u32[]{:S(2)}) copy-start(f32[12,200,25]{1,2,0:T(8,128)} %squeeze.64) | copy-start | bytes 720004
  73.5 2.3 %copy-start.6 = (f32[12,200,25]{1,2,0:T(8,128)S(1)}, f32[12,200,25]{1,2,0:T(8,128)}, u32[]{:S(2)}) copy-start(f32[12,200,25]{1,2,0:T(8,128)} %copy-done.5) | copy-start | bytes 720004
  76.9 17.2 %copy-start.7 = (f32[1,2,25,2,32,2,12]{4,5,6,3,2,1,0:T(2,128)S(1)}, f32[1,2,25,2,32,2,12]{4,5,6,3,2,1,0:T(2,128)}, u32[]{:S(2)}) copy-start(f32[1,2,25,2,32,2,12]{4,5,6,3,2,1,0:T(2,128)} %param.24) | copy-start | bytes 921604
  95.2 2.3 %copy-start.15 = (f32[4]{0:T(128)S(1)}, f32[4]{0:T(128)}, u32[]{:S(2)}) copy-start(f32[4]{0:T(128)} %param.25) | copy-start | bytes 52
  97.1 2.8 %copy-start.10 = (bf16[64,32,32]{0,2,1:T(8,128)(2,1)S(1)}, bf16[64,32,32]{0,2,1:T(8,128)(2,1)}, u32[]{:S(2)}) copy-start(bf16[64,32,32]{0,2,1:T(8,128)(2,1)} %param.27) | copy-start | bytes 393220
  97.4 3.3 %copy-start.16 = (u32[32]{0:T(128)S(1)}, u32[32]{0:T(128)}, u32[]{:S(2)}) copy-start(u32[32]{0:T(128)} %constant.84) | copy-start | bytes 388
  137.3 8.8 %all-to-all-start = ((bf16[4,2,512]{2,1,0:T(2,128)(2,1)}), bf16[4,2,512]{2,1,0:T(2,128)(2,1)S(1)}, u32[]{:S(2)}, u32[]{:S(2)}) async-start(bf16[4,2,512]{2,1,0:T(2,128)(2,1)} %reshape.377), calls=%async_computation | async-start | bytes 16384 | tf_op jit(solution)/shard_map/all_to_all | solution.py:222
Sparse Core Ops, SparseCore 0:
  100.0 22.0 reduce-scatter.3
where the time goes:
time: 173 us; the launch traced here: 170 us
  local copies, waits for them, and re-layouts  50.4 us (29%)
  matrix products  37.5 us (22%)
  waiting for transfers between devices  26.1 us (15%)
  blocking collectives  24.2 us (14%)
  between operations  15.3 us (9%)
  other arithmetic  13 us (8%)
  starting transfers between devices  3.46 us (2%)
    unnamed x2, waiting for transfers between devices  20.8 us
    dot_general x1, matrix products, synthesize(): product = jnp.dot(spectrum, table, preferred_element_type=jnp.float32)  15.7 us
    psum x1, blocking collectives, on_device(): owner_sum = lax.psum(partial_owner, ('state', 'sub'))  13.9 us
    unnamed x1, blocking collectives  10.3 us
    slice x4, local copies, waits for them, and re-layouts, turn_select(): mats[0]  8.68 us
    dot_general x4, matrix products, turn_select(): jnp.einsum('lQp,lpC->lQC', mats[1], vectors, precision=lax.Precision.HIGH...  7.41 us
    dot_general x4, matrix products, turn_select(): jnp.einsum('lQp,lpC->lQC', mats[0], vectors, precision=lax.Precision.HIGH...  7.38 us
    reshape x4, local copies, waits for them, and re-layouts, turn_select(): complex_join(first, second, width // 2).reshape(degrees, 8, orders, width)  6.15 us
  transfers between devices with their start and end apart: 2, of which 2 were waited for; matrix products, arithmetic and copies ran while one was open for 1% of the time, Pallas kernels for 0%

commit v1 on v0

--- a/solution.py
+++ b/solution.py
@@ -193,7 +193,7 @@
         axial_one,
         axial_two,
     )
-    owner_sum = lax.psum(partial_owner, ("state", "sub"))
+    owner_sum = jnp.sum(lax.all_gather(partial_owner, ("state", "sub")), axis=0)
     framed = owner_frame(owner_sum, owner_rotation[0], owner_axial[0])
     leaf_size = lax.axis_size("leaf")
     orders = turn_table.shape[3]

time: 173 us -> 168 us (0.971)
  blocking collectives: 24.2 us -> 18.2 us
    psum x1 -> x0, blocking collectives: 13.9 us -> none  [on_device(): owner_sum = lax.psum(partial_owner, ('state', 'sub'))]
    all_gather x0 -> x1, blocking collectives: none -> 7.92 us  [on_device(): owner_sum = jnp.sum(lax.all_gather(partial_owner, ('state', 'sub')), axis=0)]
where the time goes in v1:
time: 168 us; the launch traced here: 165 us
  local copies, waits for them, and re-layouts  50.4 us (30%)
  matrix products  37.5 us (22%)
  waiting for transfers between devices  26.7 us (16%)
  blocking collectives  18.2 us (11%)
  between operations  15.3 us (9%)
  other arithmetic  13 us (8%)
  starting transfers between devices  3.46 us (2%)
    unnamed x2, waiting for transfers between devices  21.4 us
    dot_general x1, matrix products, synthesize(): product = jnp.dot(spectrum, table, preferred_element_type=jnp.float32)  15.7 us
    unnamed x1, blocking collectives  10.3 us
    slice x4, local copies, waits for them, and re-layouts, turn_select(): mats[0]  8.68 us
    all_gather x1, blocking collectives, on_device(): owner_sum = jnp.sum(lax.all_gather(partial_owner, ('state', 'sub')), axis=0)  7.92 us
    dot_general x4, matrix products, turn_select(): jnp.einsum('lQp,lpC->lQC', mats[1], vectors, precision=lax.Precision.HIGH...  7.41 us
    dot_general x4, matrix products, turn_select(): jnp.einsum('lQp,lpC->lQC', mats[0], vectors, precision=lax.Precision.HIGH...  7.38 us
    reshape x4, local copies, waits for them, and re-layouts, turn_select(): complex_join(first, second, width // 2).reshape(degrees, 8, orders, width)  6.15 us
  transfers between devices with their start and end apart: 2, of which 2 were waited for; matrix products, arithmetic and copies ran while one was open for 1% of the time, Pallas kernels for 0%

profile of v1, /device:TPU:0, one launch (start us, length us, event | category | flops | bytes accessed | tf_op | source)
XLA Modules:
  0.0 164.6 jit_solution(15084361476817842665)
XLA Ops:
  6.5 0.6 fusion.33
  7.1 4.5 %fusion.46 = (f32[1,12,8,25,25]{4,0,3,1,2:T(1,128)S(1)}, f32[1,12,8,25,25]{4,0,3,1,2:T(1,128)S(1)}) fusion(f32[2,12,8,25,25]{4,0,3,1,2:T(2,128)} %bitcast.183), kind=kLoop, calls=%fused_computation.129 | loop fusion | bytes 960000 | tf_op jit(solution)/shard_map/slice | solution.py:27
  11.7 2.4 %copy.163 = f32[1,12,8,25,25]{3,2,4,1,0:T(8,128)} copy(f32[1,12,8,25,25]{4,0,3,1,2:T(1,128)S(1)} %get-tuple-element.12) | data formatting | bytes 480000 | tf_op jit(solution)/shard_map/slice | solution.py:28
  14.1 2.4 %squeeze.61 = f32[12,200,25]{1,2,0:T(8,128)} reshape(f32[1,12,8,25,25]{3,2,4,1,0:T(8,128)} %copy.163) | data formatting | bytes 480000 | tf_op jit(solution)/shard_map/squeeze | solution.py:28
  17.4 0.7 mul.178
  18.1 2.6 %reshape.344 = bf16[300,1024]{1,0:T(8,128)(2,1)S(1)} reshape(bf16[12,25,2,2,4,64]{5,4,3,2,1,0:T(4,128)(2,1)} %param.14) | data formatting | bytes 1228800 | tf_op jit(solution)/shard_map/reshape | solution.py:78
  21.2 1.1 copy.162
  22.7 3.3 %convolution_bitcast_fusion.2 = f32[12,200,256]{2,1,0:T(8,128)S(1)} fusion(f32[12,25,256]{2,1,0:T(8,128)S(1)} %reshape.345, f32[12,200,25]{1,2,0:T(8,128)} %squeeze.61), kind=kOutput, calls=%fused_computation.26 | convolution fusion | flops 184320000 | bytes 3004800 | tf_op jit(solution)/shard_map/lQp,lpC->lQC/dot_general | solution.py:28
  26.0 2.2 %convolution_bitcast_fusion.3 = f32[12,200,256]{2,1,0:T(8,128)S(1)} fusion(f32[12,25,256]{2,1,0:T(8,128)S(1)} %reshape.345, f32[12,200,25]{1,2,0:T(8,128)S(1)} %squeeze.60), kind=kOutput, calls=%fused_computation.27 | convolution fusion | flops 184320000 | bytes 3004800 | tf_op jit(solution)/shard_map/lQp,lpC->lQC/dot_general | solution.py:27
  28.4 1.6 pad_maximum_fusion
  30.1 2.5 %reshape.346 = f32[12,8,25,256]{3,2,1,0:T(8,128)S(1)} reshape(f32[12,200,256]{2,1,0:T(8,128)} %pad_maximum_fusion) | data formatting | bytes 4915200 | tf_op jit(solution)/shard_map/reshape | solution.py:29
  32.5 0.7 fusion.37
  33.2 0.6 tile.8
  33.8 1.5 tile.9
  35.4 1.9 %multiply_reduce_fusion.1 = f32[12,25,256]{2,1,0:T(8,128)} fusion(f32[12,8,25,256]{3,2,1,0:T(8,128)S(1)} %reshape.346, f32[8,256]{1,0:T(8,128)} %tile.9), kind=kLoop, calls=%fused_computation.13 | loop fusion | flops 1152000 | bytes 2772992 | tf_op jit(solution)/shard_map/reduce_sum | solution.py:33
  37.2 1.4 reshape.347
  39.4 0.7 copy.206
  40.4 1.1 copy.205
  41.8 0.6 convolution_bitcast_fusion.8
  42.5 0.6 convolution_bitcast_fusion.9
  43.5 1.2 reshape.349
  44.7 2.2 %copy.169 = f32[12,25,2,2,64]{4,3,2,1,0:T(2,128)} copy(f32[12,25,2,2,64]{4,2,0,3,1:T(2,128)} %bitcast.185) | data formatting | bytes 614400 | tf_op jit(solution)/shard_map/transpose | solution.py:45
  46.9 1.5 reshape.350
  48.4 2.9 %fusion.45 = (f32[1,12,8,25,25]{3,0,4,1,2:T(1,128)S(1)}, f32[1,12,8,25,25]{3,0,4,1,2:T(1,128)}) fusion(f32[2,12,8,25,25]{3,0,4,1,2:T(2,128)S(1)} %bitcast.184), kind=kLoop, calls=%fused_computation.128 | loop fusion | bytes 960000 | tf_op jit(solution)/shard_map/slice | solution.py:27
  51.5 1.1 squeeze.64
  53.1 3.3 %convolution_bitcast_fusion.1 = f32[12,200,256]{2,1,0:T(8,128)S(1)} fusion(f32[12,25,256]{2,1,0:T(8,128)S(1)} %reshape.350, f32[12,200,25]{1,2,0:T(8,128)} %squeeze.64), kind=kOutput, calls=%fused_computation.25 | convolution fusion | flops 184320000 | bytes 3004800 | tf_op jit(solution)/shard_map/lQp,lpC->lQC/dot_general | solution.py:27
  56.5 2.2 %multiply_bitcast_fusion = f32[12,200,256]{2,1,0:T(8,128)S(1)} fusion(f32[12,25,256]{2,1,0:T(8,128)S(1)} %reshape.350, f32[12,200,25]{1,2,0:T(8,128)S(1)} %squeeze.65), kind=kOutput, calls=%fused_computation.16 | convolution fusion | flops 184934400 | bytes 3004800 | tf_op jit(solution)/shard_map/lQp,lpC->lQC/dot_general | solution.py:28
  58.9 1.6 pad_maximum_fusion.1
  60.5 2.6 %reshape.351 = f32[12,8,25,256]{3,2,1,0:T(8,128)S(1)} reshape(f32[12,200,256]{2,1,0:T(8,128)} %pad_maximum_fusion.1) | data formatting | bytes 4915200 | tf_op jit(solution)/shard_map/reshape | solution.py:29
  63.2 1.9 %multiply_reduce_fusion = f32[12,25,256]{2,1,0:T(8,128)} fusion(f32[12,8,25,256]{3,2,1,0:T(8,128)S(1)} %reshape.351, f32[8,256]{1,0:T(8,128)} %tile.9), kind=kLoop, calls=%fused_computation.12 | loop fusion | flops 1152000 | bytes 2772992 | tf_op jit(solution)/shard_map/reduce_sum | solution.py:33
  65.3 2.0 %fusion.51 = f32[12,25,32]{1,2,0:T(8,128)S(1)} fusion(f32[12,25,256]{2,1,0:T(8,128)} %multiply_reduce_fusion, f32[256,32,1]{0,1,2:T(8,128)S(1)} %reshape.366), kind=kOutput, calls=%fused_computation.136 | convolution fusion | flops 29491200 | bytes 378368 | tf_op jit(solution)/shard_map/lpC,CD->lpD/dot_general | solution.py:91
  67.3 1.5 convolution_bitcast_fusion.6
  68.8 1.5 convolution_bitcast_fusion.5
  70.4 0.5 reshape.352
  71.0 0.5 multiply_reduce_fusion.3
  71.8 0.7 copy.208
  72.8 0.7 copy.207
  73.8 0.6 convolution_bitcast_fusion.10
  74.4 0.6 convolution_bitcast_fusion.11
  75.3 0.5 convolution_bitcast_fusion.4
  75.8 0.5 fusion.15
  76.4 0.5 reshape.357
  76.9 0.5 multiply_reduce_fusion.2
  77.7 7.9 %all-gather = f32[48,25,16]{1,2,0:T(8,128)S(1)} all-gather(f32[12,25,16]{1,2,0:T(8,128)S(1)} %reduce_sum.58), channel_id=2, replica_groups=mesh['groups'=2,'leaf'=4,'state'=2,'sub'=2] {'state','sub'}, dimensions={0}, use_global_device_ids=true | all-gather | bytes 96000 | tf_op jit(solution)/shard_map/all_gather | solution.py:196
  85.6 1.4 fusion.50
  87.0 0.4 convolution_bitcast_fusion.14
  87.4 0.4 convolution_bitcast_fusion.15
  89.9 0.4 convolution_bitcast_fusion.13
  91.5 0.6 dynamic_slice.3
  92.1 0.7 fusion.38
  92.9 1.0 copy.210
  93.9 0.8 copy.195
  94.7 0.6 dynamic-slice
  95.3 21.3 %reduce-scatter.4.cloned.1.call-done = f32[64,512]{1,0:T(8,128)} async-done(((f32[256,512]{1,0:T(8,128)}), f32[64,512]{1,0:T(8,128)}) %reduce-scatter.4.cloned.1.call-update) | async-done | bytes 131088
  116.7 1.0 copy.211
  119.1 10.3 %all-reduce = bf16[4,4,1024]{2,1,0:T(4,128)(2,1)S(1)} all-reduce(bf16[4,4,1024]{2,1,0:T(4,128)(2,1)S(1)} %copy.209), channel_id=4, replica_groups=mesh['groups'=2,'leaf'=4,'state'=2,'sub'=2] {'state','sub'}, use_global_device_ids=true, to_apply=%region_7.8.clone | all-reduce | flops 16384 | bytes 65536
  129.3 0.7 constant_dynamic-slice_fusion
  130.0 0.5 broadcast.208
  130.6 0.7 reduce.2
  131.2 0.6 reshape.378
  131.9 3.5 %all-to-all-start = ((bf16[4,2,512]{2,1,0:T(2,128)(2,1)}), bf16[4,2,512]{2,1,0:T(2,128)(2,1)S(1)}, u32[]{:S(2)}, u32[]{:S(2)}) async-start(bf16[4,2,512]{2,1,0:T(2,128)(2,1)} %reshape.378), calls=%async_computation | async-start | bytes 16384 | tf_op jit(solution)/shard_map/all_to_all | solution.py:222
  135.3 5.3 %all-to-all-done = bf16[4,2,512]{2,1,0:T(2,128)(2,1)S(1)} async-done(((bf16[4,2,512]{2,1,0:T(2,128)(2,1)}), bf16[4,2,512]{2,1,0:T(2,128)(2,1)S(1)}, u32[]{:S(2)}, u32[]{:S(2)}) %all-to-all-start) | async-done | bytes 8224 | tf_op jit(solution)/shard_map/all_to_all | solution.py:222
  140.9 15.7 %convolution_bitcast_fusion = f32[2,2,4,1,4096]{4,2,1,0,3:T(4,128)S(1)} fusion(bf16[2,2,4,256]{3,2,1,0:T(4,128)(2,1)S(1)} %dot_general.132, f32[4096]{0:T(1024)S(1)} %fusion.28, s32[4096]{0:T(1024)S(1)} %add_select_fusion.2, s32[256]{0:T(256)S(1)} %iota_add_fusion), kind=kOutput, calls=%fused_computation.5 | convolution fusion | flops 50331648 | bytes 304128 | tf_op jit(solution)/shard_map/dot_general | solution.py:161
  156.7 0.8 copy.202
  (114 shorter events, 10.7 us)
Async XLA Ops:
  6.5 84.2 %copy-start = (bf16[1,32,25,256]{3,1,2,0:T(8,128)(2,1)S(1)}, bf16[1,32,25,256]{3,1,2,0:T(8,128)(2,1)}, u32[]{:S(2)}) copy-start(bf16[1,32,25,256]{3,1,2,0:T(8,128)(2,1)} %param.26) | copy-start | bytes 1228804
  6.5 110.1 %reduce-scatter.4.cloned.1.call-start = ((), (), s32[]{:S(2)}) async-start(), calls=%async_computation.2 | async-start | bytes 655360
  11.7 5.5 %copy-start.12 = (s32[64]{0:T(128)S(1)}, s32[64]{0:T(128)}, u32[]{:S(2)}) copy-start(s32[64]{0:T(128)} %param.16) | copy-start | bytes 772
  22.7 5.5 %copy-start.3 = (f32[12,200,25]{1,2,0:T(8,128)}, f32[12,200,25]{1,2,0:T(8,128)S(1)}, u32[]{:S(2)}) copy-start(f32[12,200,25]{1,2,0:T(8,128)S(1)} %squeeze.60) | copy-start | bytes 720004
  37.2 2.1 %copy-start.8 = (f32[2,25,2,12,2,12]{1,4,5,3,2,0:T(2,128)S(1)}, f32[2,25,2,12,2,12]{1,4,5,3,2,0:T(2,128)}, u32[]{:S(2)}) copy-start(f32[2,25,2,12,2,12]{1,4,5,3,2,0:T(2,128)} %param.21) | copy-start | bytes 345604
  43.3 5.1 %copy-start.1 = (f32[8,2,12,25,25]{4,1,3,2,0:T(2,128)S(1)}, f32[8,2,12,25,25]{4,1,3,2,0:T(2,128)}, u32[]{:S(2)}) copy-start(f32[8,2,12,25,25]{4,1,3,2,0:T(2,128)} %param.20) | copy-start | bytes 1440004
  51.4 1.3 copy-start.2
  53.1 5.5 %copy-start.5 = (f32[12,200,25]{1,2,0:T(8,128)}, f32[12,200,25]{1,2,0:T(8,128)S(1)}, u32[]{:S(2)}) copy-start(f32[12,200,25]{1,2,0:T(8,128)S(1)} %squeeze.65) | copy-start | bytes 720004
  63.2 1.9 %copy-start.13 = (s32[16]{0:T(128)S(1)}, s32[16]{0:T(128)}, u32[]{:S(2)}) copy-start(s32[16]{0:T(128)} %param.17) | copy-start | bytes 196
  63.2 1.9 %copy-start.11 = (f32[16,16]{0,1:T(8,128)S(1)}, f32[16,16]{0,1:T(8,128)}, u32[]{:S(2)}) copy-start(f32[16,16]{0,1:T(8,128)} %fusion.33) | copy-start | bytes 3076
  68.8 2.1 %copy-start.14 = (s32[2]{0:T(128)S(1)}, s32[2]{0:T(128)}, u32[]{:S(2)}) copy-start(s32[2]{0:T(128)} %param.19) | copy-start | bytes 28
  70.4 1.4 copy-start.9
  72.8 2.5 %copy-start.4 = (f32[12,200,25]{1,2,0:T(8,128)S(1)}, f32[12,200,25]{1,2,0:T(8,128)}, u32[]{:S(2)}) copy-start(f32[12,200,25]{1,2,0:T(8,128)} %squeeze.64) | copy-start | bytes 720004
  73.5 2.3 %copy-start.6 = (f32[12,200,25]{1,2,0:T(8,128)S(1)}, f32[12,200,25]{1,2,0:T(8,128)}, u32[]{:S(2)}) copy-start(f32[12,200,25]{1,2,0:T(8,128)} %copy-done.5) | copy-start | bytes 720004
  76.9 11.2 %copy-start.7 = (f32[1,2,25,2,32,2,12]{4,5,6,3,2,1,0:T(2,128)S(1)}, f32[1,2,25,2,32,2,12]{4,5,6,3,2,1,0:T(2,128)}, u32[]{:S(2)}) copy-start(f32[1,2,25,2,32,2,12]{4,5,6,3,2,1,0:T(2,128)} %param.24) | copy-start | bytes 921604
  89.2 2.3 %copy-start.15 = (f32[4]{0:T(128)S(1)}, f32[4]{0:T(128)}, u32[]{:S(2)}) copy-start(f32[4]{0:T(128)} %param.25) | copy-start | bytes 52
  91.1 2.8 %copy-start.10 = (bf16[64,32,32]{0,2,1:T(8,128)(2,1)S(1)}, bf16[64,32,32]{0,2,1:T(8,128)(2,1)}, u32[]{:S(2)}) copy-start(bf16[64,32,32]{0,2,1:T(8,128)(2,1)} %param.27) | copy-start | bytes 393220
  91.4 3.3 %copy-start.16 = (u32[32]{0:T(128)S(1)}, u32[32]{0:T(128)}, u32[]{:S(2)}) copy-start(u32[32]{0:T(128)} %constant.84) | copy-start | bytes 388
  131.9 8.8 %all-to-all-start = ((bf16[4,2,512]{2,1,0:T(2,128)(2,1)}), bf16[4,2,512]{2,1,0:T(2,128)(2,1)S(1)}, u32[]{:S(2)}, u32[]{:S(2)}) async-start(bf16[4,2,512]{2,1,0:T(2,128)(2,1)} %reshape.378), calls=%async_computation | async-start | bytes 16384 | tf_op jit(solution)/shard_map/all_to_all | solution.py:222
Sparse Core Ops, SparseCore 0:
  94.0 22.5 reduce-scatter.3
